TPU v7x, 512 devices: a whole 4x4x16 slice. The times are simulated.
512 devices in a mesh: req: 32 (over y, x, core), mlp: 16 (over z).
Axes of the slice: x: 4, y: 4, z: 16, core: 2. Of those that a mesh axis runs over, the one named last changes fastest.
Arguments:
- queries: bfloat16 [12288, 4096], P('req', 'mlp')
- new_keys: bfloat16 [12288, 1024], P(('req', 'mlp')), may hold values from -5 to 5
- new_values: bfloat16 [12288, 1024], P(('req', 'mlp')), may hold values from -6 to 6
- cache_keys: bfloat16 [32, 4096, 1024], P('req', 'mlp')
- cache_values: bfloat16 [32, 4096, 1024], P('req', 'mlp'), may hold values from -6 to 6
- cache_len: int32 [32], P('req'), may hold values from 256 to 4096, as said below
- residual: bfloat16 [12288, 2560], P('req')
- out_weight: bfloat16 [4096, 2560], P('mlp'), may hold values from -0.1796875 to 0.1796875
- norm_gain: bfloat16 [2560], replicated, may hold values from 0.099609375 to 1.8984375
- gate_weight: bfloat16 [2560, 9728], P('req', 'mlp'), may hold values from -0.125 to 0.125
- up_weight: bfloat16 [2560, 9728], P('req', 'mlp'), may hold values from -0.125 to 0.125
- down_weight: bfloat16 [2560, 9728], P('req', 'mlp'), may hold values from -0.0625 to 0.0625
Outputs:
- layer_out: bfloat16 [12288, 2560], P(('req', 'mlp'))
Inputs may be any that keep to these rules, and one draw needn't show every extreme that they name: cache_len[r] counts request r's valid cached positions from the first; some request has exactly 4096.
All inputs are finite; a program needn't handle non-finite values.
Results may differ from a plain program's by a relative error of at most 0.012.
Values may be sent and summed in bfloat16 or wider, within the bound.
No kernel may reach another device: no remote copies, remote signals or barrier semaphores. Data moves between devices by JAX's collectives and lax.ppermute only.
A program may use at most 64 MiB of HBM per device.

v0:
```python
import jax
import jax.numpy as jnp
from jax import lax
from jax.sharding import PartitionSpec as P

H = 32
KVH = 8
HD = 128
norm_eps = 1e-06


def shards(
    queries,
    new_keys,
    new_values,
    cache_keys,
    cache_values,
    cache_len,
    residual,
    out_weight,
    norm_gain,
    gate_weight,
    up_weight,
    down_weight,
):
    n_mlp = lax.axis_size("mlp")
    heads_dev = H // n_mlp
    group_size = H // KVH
    copies = n_mlp // KVH
    assert copies == 2 and heads_dev * copies == group_size
    query_rows = queries.shape[0]
    rows_dev = new_keys.shape[0]
    cache_dev = cache_keys.shape[1]
    cache_half = cache_dev // copies
    new_half = rows_dev // copies
    my_index = lax.axis_index("mlp")
    my_half = my_index % copies

    def to_slots(rows_block, half_rows):
        spread = rows_block.reshape(copies, half_rows, KVH, HD).transpose(1, 2, 0, 3)
        return spread.reshape(half_rows, KVH * copies, HD)

    send = jnp.concatenate(
        [
            to_slots(cache_keys[0], cache_half),
            to_slots(cache_values[0], cache_half),
            to_slots(new_keys, new_half),
            to_slots(new_values, new_half),
        ],
        axis=0,
    )
    arrived = lax.all_to_all(send, "mlp", split_axis=1, concat_axis=0, tiled=True)
    per_src = 2 * cache_half + 2 * new_half
    arrived = arrived.reshape(n_mlp, per_src, HD)
    keys_old = arrived[:, :cache_half].reshape(n_mlp * cache_half, HD)
    values_old = arrived[:, cache_half : 2 * cache_half].reshape(n_mlp * cache_half, HD)
    keys_new = arrived[:, 2 * cache_half : 2 * cache_half + new_half].reshape(n_mlp * new_half, HD)
    values_new = arrived[:, 2 * cache_half + new_half :].reshape(n_mlp * new_half, HD)
    pair = [(d, d ^ 1) for d in range(n_mlp)]
    partner_q = lax.ppermute(queries, "mlp", pair)
    grouped = jnp.concatenate([queries, partner_q], axis=1).reshape(query_rows, group_size, HD)
    score_scale = HD ** (-0.5)
    length = cache_len[0]
    cache_count = n_mlp * cache_half
    keys_all = jnp.concatenate([keys_old, keys_new], axis=0)
    values_all = jnp.concatenate([values_old, values_new], axis=0)
    cached_idx = lax.iota(jnp.int32, cache_count)
    cached_pos = (
        cached_idx // cache_half * cache_dev + my_half * cache_half + cached_idx % cache_half
    )
    new_idx = lax.iota(jnp.int32, n_mlp * new_half)
    new_pos = new_idx // new_half * rows_dev + my_half * new_half + new_idx % new_half
    token_ids = lax.iota(jnp.int32, query_rows)
    allowed = jnp.concatenate(
        [
            jnp.broadcast_to((cached_pos < length)[None, :], (query_rows, cache_count)),
            new_pos[None, :] <= token_ids[:, None],
        ],
        axis=1,
    )
    scores = (
        jnp.einsum("tqd,kd->qtk", grouped, keys_all, preferred_element_type=jnp.float32)
        * score_scale
    )
    scores = jnp.where(allowed[None], scores, -jnp.inf)
    row_max = jnp.max(scores, axis=-1)
    weights = jnp.exp(scores - row_max[..., None])
    row_sum = jnp.sum(weights, axis=-1)
    weighted = jnp.einsum(
        "qtk,kd->qtd", weights.astype(jnp.bfloat16), values_all, preferred_element_type=jnp.float32
    )
    sent = lax.ppermute(
        (weighted[heads_dev:], row_max[heads_dev:], row_sum[heads_dev:]), "mlp", pair
    )
    other_weighted, other_max, other_sum = sent
    mine_max = row_max[:heads_dev]
    top = jnp.maximum(mine_max, other_max)
    scale_a = jnp.exp(mine_max - top)
    scale_b = jnp.exp(other_max - top)
    total = row_sum[:heads_dev] * scale_a + other_sum * scale_b
    mixed = weighted[:heads_dev] * scale_a[..., None] + other_weighted * scale_b[..., None]
    attended = (mixed / total[..., None]).astype(jnp.bfloat16)
    attended = attended.transpose(1, 0, 2).reshape(query_rows, heads_dev * HD)
    partial_value = jnp.dot(attended, out_weight, preferred_element_type=jnp.float32)
    row_start = my_index * rows_dev
    head_sum = lax.psum(partial_value.astype(jnp.bfloat16), "mlp").astype(jnp.float32)
    stream = (residual.astype(jnp.float32) + head_sum).astype(jnp.bfloat16)
    stream_full = stream.astype(jnp.float32)
    factor = lax.rsqrt(jnp.mean(stream_full * stream_full, axis=-1, keepdims=True) + norm_eps)
    normed = (stream_full * factor * norm_gain.astype(jnp.float32)).astype(jnp.bfloat16)
    stream_rows = lax.dynamic_slice_in_dim(stream, row_start, rows_dev, 0)
    units = gate_weight.shape[1]
    width = -(-units // 128) * 128

    def padded(block):
        return jnp.pad(block, ((0, 0), (0, width - units)))

    weights_full = lax.all_gather(
        jnp.concatenate([padded(gate_weight), padded(up_weight), padded(down_weight)], axis=1),
        "req",
        axis=0,
        tiled=True,
    )
    both = jnp.dot(normed, weights_full[:, : 2 * width], preferred_element_type=jnp.float32)
    gate_sum = both[:, :width]
    up_sum = both[:, width:]
    hidden = (jax.nn.silu(gate_sum) * up_sum).astype(jnp.bfloat16)
    mlp_part = lax.dot_general(
        hidden,
        weights_full[:, 2 * width :],
        (((1,), (1,)), ((), ())),
        preferred_element_type=jnp.float32,
    )
    mlp_rows = lax.psum_scatter(
        mlp_part.astype(jnp.bfloat16), "mlp", scatter_dimension=0, tiled=True
    ).astype(jnp.float32)
    return (stream_rows.astype(jnp.float32) + mlp_rows).astype(jnp.bfloat16)


def solution(mesh):
    in_specs = (
        P("req", "mlp"),
        P(("req", "mlp"), None),
        P(("req", "mlp"), None),
        P("req", "mlp", None),
        P("req", "mlp", None),
        P("req"),
        P("req", None),
        P("mlp", None),
        P(),
        P("req", "mlp"),
        P("req", "mlp"),
        P("req", "mlp"),
    )
    out_specs = P(("req", "mlp"), None)
    return jax.shard_map(shards, mesh=mesh, in_specs=in_specs, out_specs=out_specs, check_vma=False)
```

profile of v0, /device:TPU:8, one launch (start us, length us, event | category | flops | bytes accessed | tf_op | source)
XLA Modules:
  0.0 349.7 jit_solution(10881288263603468844)
XLA Ops:
  7.4 1.3 copy.25
  9.2 1.1 pad_maximum_fusion
  10.3 15.2 %all-to-all-start = ((bf16[280,16,128]{2,0,1:T(8,128)(2,1)}), bf16[280,16,128]{2,0,1:T(8,128)(2,1)S(1)}, u32[]{:S(2)}, u32[]{:S(2)}) async-start(bf16[280,16,128]{2,0,1:T(8,128)(2,1)} %pad_maximum_fusion), calls=%async_computation | async-start | bytes 2293760 | tf_op jit(solution)/shard_map/all_to_all | solution.py:52
  25.7 3.8 %collective-permute-start = (bf16[384,256]{0,1:T(8,128)(2,1)S(1)}, bf16[384,256]{0,1:T(8,128)(2,1)}, u32[]{:S(2)}, u32[]{:S(2)}) collective-permute-start(bf16[384,256]{0,1:T(8,128)(2,1)S(1)} %copy.22), channel_id=1, source_target_pairs={{0,1},{1,0},{2,3},{3,2},{4,5},{5,4},{6,7},{7,6},{8,9},{9,8},{10,11... | collective-permute-start | bytes 589832 | tf_op jit(solution)/shard_map/ppermute | solution.py:60
  30.4 2.1 pad_add_fusion
  32.5 48.9 %collective-permute-done = bf16[384,256]{0,1:T(8,128)(2,1)} collective-permute-done((bf16[384,256]{0,1:T(8,128)(2,1)S(1)}, bf16[384,256]{0,1:T(8,128)(2,1)}, u32[]{:S(2)}, u32[]{:S(2)}) %collective-permute-start) | collective-permute-done | bytes 196640 | tf_op jit(solution)/shard_map/ppermute | solution.py:60
  81.4 1.7 pad_maximum_fusion.1
  83.1 1.1 fusion.58
  84.3 4.0 %fusion.2 = (f32[4,384]{1,0:T(4,128)S(1)}, f32[2240,384,4]{1,0,2:T(8,128)S(1)}) fusion(pred[384,2240]{0,1:T(8,128)(4,1)S(1)} %pad_add_fusion, bf16[384,4,128]{0,2,1:T(8,128)(2,1)} %bitcast.74, bf16[192,128]{1,0:T(8,128)(2,1)S(1)} %reshape.106, bf16[2048,128]{1,0:T(8,128)(2,1)} %bitcast.73), kind=kOutput, calls=%fused_computation.4 | convolution fusion | flops 892271104 | bytes 15595520 | tf_op jit(solution)/shard_map/tqd,kd->qtk/dot_general | solution.py:82
  88.4 3.3 fusion.3
  91.7 1.6 copy-done.1
  93.4 2.2 collective-permute-start.2
  95.6 7.8 %fusion = f32[4,384]{1,0:T(4,128)S(1)} fusion(f32[2240,384,4]{1,0,2:T(8,128)} %copy-done.1, f32[4,384]{1,0:T(4,128)S(1)} %get-tuple-element.14, pred[384,2240]{0,1:T(8,128)(4,1)S(1)} %pad_add_fusion), kind=kLoop, calls=%fused_computation.2 | loop fusion | flops 13761024 | bytes 14635008 | tf_op jit(solution)/shard_map/reduce_sum | solution.py:88
  103.4 3.6 %collective-permute-start.3 = (f32[2,384]{1,0:T(2,128)S(1)}, f32[2,384]{1,0:T(2,128)S(1)}, u32[]{:S(2)}, u32[]{:S(2)}) collective-permute-start(f32[2,384]{1,0:T(2,128)S(1)} %slice.65), channel_id=1, source_target_pairs={{0,1},{1,0},{2,3},{3,2},{4,5},{5,4},{6,7},{7,6},{8,9},{9,8},{10,11... | collective-permute-start | bytes 9224 | tf_op jit(solution)/shard_map/ppermute | solution.py:92
  107.1 2.2 collective-permute-start.1
  109.3 3.2 collective-permute-done.1
  112.7 2.1 convolution_convert_fusion.1
  114.9 0.8 fusion.31
  115.9 142.1 %all-reduce.5.cloned.1.call-done = bf16[384,2560]{1,0:T(8,128)(2,1)} async-done(((bf16[384,2560]{1,0:T(8,128)(2,1)}), bf16[384,2560]{1,0:T(8,128)(2,1)}) %all-reduce.5.cloned.1.call-update) | async-done | bytes 1966096 | tf_op jit(solution)/shard_map/psum | solution.py:106
  258.0 3.0 fusion.8
  261.0 5.6 %fusion.6 = f32[384,1280]{1,0:T(8,128)S(1)} fusion(bf16[2560,1920]{1,0:T(8,128)(2,1)} %all-gather.2.cloned.1.call-done, bf16[384,2560]{1,0:T(8,128)(2,1)S(1)} %get-tuple-element.6, f32[2560]{0:T(1024)S(1)} %convert_element_type.54, f32[384]{0:T(512)S(1)} %add_rsqrt_fusion), kind=kOutput, calls=%fused_computation.7 | convolution fusion | flops 2520514560 | bytes 10497536 | tf_op jit(solution)/shard_map/dot_general | solution.py:124
  266.6 5.0 %convolution_convert_fusion = bf16[384,2560]{1,0:T(8,128)(2,1)} fusion(bf16[2560,1920]{1,0:T(8,128)(2,1)} %all-gather.2.cloned.1.call-done, f32[384,1280]{1,0:T(8,128)S(1)} %fusion.6), kind=kOutput, calls=%fused_computation.11 | convolution fusion | flops 1260748800 | bytes 7208960 | tf_op jit(solution)/shard_map/dot_general | solution.py:128
  271.6 69.1 %reduce-scatter.2.cloned.1.call-done = bf16[24,2560]{1,0:T(8,128)(2,1)} async-done(((bf16[384,2560]{1,0:T(8,128)(2,1)}), bf16[24,2560]{1,0:T(8,128)(2,1)}) %reduce-scatter.2.cloned.1.call-update) | async-done | bytes 122896 | tf_op jit(solution)/shard_map/reduce_scatter | solution.py:134
  340.7 1.6 add_convert_fusion.1
  (55 shorter events, 1.3 us)
Async XLA Ops:
  7.4 105.3 %copy-start = (bf16[256,2560]{1,0:T(8,128)(2,1)S(1)}, bf16[256,2560]{1,0:T(8,128)(2,1)}, u32[]{:S(2)}) copy-start(bf16[256,2560]{1,0:T(8,128)(2,1)} %param.19) | copy-start | bytes 3932164
  7.4 1.4 copy-start.2
  7.4 1.7 copy-start.8
  7.4 1.7 copy-start.9
  8.9 16.6 %copy-start.4 = (bf16[384,256]{1,0:T(8,128)(2,1)S(1)}, bf16[384,256]{1,0:T(8,128)(2,1)}, u32[]{:S(2)}) copy-start(bf16[384,256]{1,0:T(8,128)(2,1)} %param.12) | copy-start | bytes 589828
  10.3 72.8 %all-to-all-start = ((bf16[280,16,128]{2,0,1:T(8,128)(2,1)}), bf16[280,16,128]{2,0,1:T(8,128)(2,1)S(1)}, u32[]{:S(2)}, u32[]{:S(2)}) async-start(bf16[280,16,128]{2,0,1:T(8,128)(2,1)} %pad_maximum_fusion), calls=%async_computation | async-start | bytes 2293760 | tf_op jit(solution)/shard_map/all_to_all | solution.py:52
  25.5 232.5 %all-reduce.5.cloned.1.call-start = ((), (), s32[]{:S(2)}) async-start(), calls=%async_computation.2 | async-start | bytes 3932160 | tf_op jit(solution)/shard_map/psum | solution.py:106
  25.7 55.7 %collective-permute-start = (bf16[384,256]{0,1:T(8,128)(2,1)S(1)}, bf16[384,256]{0,1:T(8,128)(2,1)}, u32[]{:S(2)}, u32[]{:S(2)}) collective-permute-start(bf16[384,256]{0,1:T(8,128)(2,1)S(1)} %copy.22), channel_id=1, source_target_pairs={{0,1},{1,0},{2,3},{3,2},{4,5},{5,4},{6,7},{7,6},{8,9},{9,8},{10,11... | collective-permute-start | bytes 589832 | tf_op jit(solution)/shard_map/ppermute | solution.py:60
  84.3 4.1 %copy-start.3 = (bf16[16,128,128]{2,1,0:T(8,128)(2,1)S(1)}, bf16[16,128,128]{2,1,0:T(8,128)(2,1)}, u32[]{:S(2)}) copy-start(bf16[16,128,128]{2,1,0:T(8,128)(2,1)} %get-tuple-element.10) | copy-start | bytes 1572868
  88.4 5.0 %copy-start.1 = (f32[2240,384,4]{1,0,2:T(8,128)}, f32[2240,384,4]{1,0,2:T(8,128)S(1)}, u32[]{:S(2)}) copy-start(f32[2240,384,4]{1,0,2:T(8,128)S(1)} %get-tuple-element.15) | copy-start | bytes 41287684
  93.4 19.2 %collective-permute-start.2 = (f32[2,384,128]{1,2,0:T(8,128)S(1)}, f32[2,384,128]{1,2,0:T(8,128)S(1)}, u32[]{:S(2)}, u32[]{:S(2)}) collective-permute-start(f32[2,384,128]{1,2,0:T(8,128)S(1)} %slice.63), channel_id=1, source_target_pairs={{0,1},{1,0},{2,3},{3,2},{4,5},{5,4},{6,7},{7,6},{8,9},{9,8},{10,11... | collective-permute-start | bytes 1179656 | tf_op jit(solution)/shard_map/ppermute | solution.py:92
  103.4 5.9 %collective-permute-start.3 = (f32[2,384]{1,0:T(2,128)S(1)}, f32[2,384]{1,0:T(2,128)S(1)}, u32[]{:S(2)}, u32[]{:S(2)}) collective-permute-start(f32[2,384]{1,0:T(2,128)S(1)} %slice.65), channel_id=1, source_target_pairs={{0,1},{1,0},{2,3},{3,2},{4,5},{5,4},{6,7},{7,6},{8,9},{9,8},{10,11... | collective-permute-start | bytes 9224 | tf_op jit(solution)/shard_map/ppermute | solution.py:92
  107.1 5.5 %collective-permute-start.1 = (f32[2,384]{1,0:T(2,128)S(1)}, f32[2,384]{1,0:T(2,128)S(1)}, u32[]{:S(2)}, u32[]{:S(2)}) collective-permute-start(f32[2,384]{1,0:T(2,128)S(1)} %slice.62), channel_id=1, source_target_pairs={{0,1},{1,0},{2,3},{3,2},{4,5},{5,4},{6,7},{7,6},{8,9},{9,8},{10,11... | collective-permute-start | bytes 9224 | tf_op jit(solution)/shard_map/ppermute | solution.py:92
  112.6 2.3 copy-start.5
  112.6 2.3 copy-start.6
  112.6 2.3 copy-start.7
  112.7 3.2 copy-start.10
  114.8 146.2 %all-gather.2.cloned.1.call-start = ((), (), s32[]{:S(2)}) async-start(), calls=%async_computation.3 | async-start | bytes 10137600 | tf_op jit(solution)/shard_map/all_gather | solution.py:118
  115.7 225.0 %reduce-scatter.2.cloned.1.call-start = ((), (), s32[]{:S(2)}) async-start(), calls=%async_computation.4 | async-start | bytes 2088960 | tf_op jit(solution)/shard_map/reduce_scatter | solution.py:134
Sparse Core Ops, SparseCore 0:
  114.9 143.0 all-reduce.4
  271.8 68.8 reduce-scatter.1
Sparse Core Ops, SparseCore 1:
  119.0 70.9 all-gather.1
where the time goes:
time: 350 us
  waiting for transfers between devices  263 us (75%)
  starting transfers between devices  27.4 us (8%)
  matrix products  20 us (6%)
  other arithmetic  18.4 us (5%)
  between operations  15.9 us (5%)
  local copies, waits for them, and re-layouts  4.71 us (1%)
    psum x1, waiting for transfers between devices, shards(): lax.psum(partial_value.astype(jnp.bfloat16), 'mlp').astype(jnp.float32)  142 us
    reduce_scatter x1, waiting for transfers between devices, shards(): lax.psum_scatter(mlp_part.astype(jnp.bfloat16), 'mlp', scatter_dimension=...  69.1 us
    ppermute x1, waiting for transfers between devices, shards(): partner_q = lax.ppermute(queries, 'mlp', pair)  48.9 us
    all_to_all x1, starting transfers between devices, shards(): lax.all_to_all(send, 'mlp', split_axis=1, concat_axis=0, tiled=True)  15.2 us
    ppermute x3, starting transfers between devices, shards(): lax.ppermute((weighted[heads_dev:], row_max[heads_dev:], row_sum[heads_de...  8.08 us
    reduce_sum x1, other arithmetic, shards(): row_sum = jnp.sum(weights, axis=-1)  7.81 us
  transfers between devices with their start and end apart: 8, of which 4 were waited for; matrix products, arithmetic and copies ran while one was open for 5% of the time, Pallas kernels for 0%

commit v1 on v0

--- a/solution.py
+++ b/solution.py
@@ -7,6 +7,12 @@
 KVH = 8
 HD = 128
 norm_eps = 1e-06
+
+
+def gather_and_add(x, mesh_axis):
+    pieces = lax.all_gather(x, mesh_axis, axis=0, tiled=False)
+    acc = pieces.sum(axis=0)
+    return acc
 
 
 def shards(
@@ -103,7 +109,7 @@
     attended = attended.transpose(1, 0, 2).reshape(query_rows, heads_dev * HD)
     partial_value = jnp.dot(attended, out_weight, preferred_element_type=jnp.float32)
     row_start = my_index * rows_dev
-    head_sum = lax.psum(partial_value.astype(jnp.bfloat16), "mlp").astype(jnp.float32)
+    head_sum = gather_and_add(partial_value.astype(jnp.bfloat16), "mlp").astype(jnp.float32)
     stream = (residual.astype(jnp.float32) + head_sum).astype(jnp.bfloat16)
     stream_full = stream.astype(jnp.float32)
     factor = lax.rsqrt(jnp.mean(stream_full * stream_full, axis=-1, keepdims=True) + norm_eps)

time: 350 us -> 617 us (1.76)
  the two profiles are of different devices: /device:TPU:8 before, /device:TPU:2 now
where the time goes in v1:
time: 617 us; the launch traced here: 616 us
  waiting for transfers between devices  519 us (84%)
  other arithmetic  30.4 us (5%)
  starting transfers between devices  27.4 us (4%)
  matrix products  20.6 us (3%)
  between operations  14.2 us (2%)
    all_gather x1, waiting for transfers between devices, gather_and_add(): pieces = lax.all_gather(x, mesh_axis, axis=0, tiled=False)  336 us
    reduce_scatter x1, waiting for transfers between devices, shards(): lax.psum_scatter(mlp_part.astype(jnp.bfloat16), 'mlp', scatter_dimension=...  72.7 us
    all_gather x1, waiting for transfers between devices, shards(): lax.all_gather(jnp.concatenate([padded(gate_weight), padded(up_weight), p...  57.8 us
    ppermute x1, waiting for transfers between devices, shards(): partner_q = lax.ppermute(queries, 'mlp', pair)  48.9 us
    all_to_all x1, starting transfers between devices, shards(): lax.all_to_all(send, 'mlp', split_axis=1, concat_axis=0, tiled=True)  15.2 us
  transfers between devices with their start and end apart: 8, of which 5 were waited for; matrix products, arithmetic and copies ran while one was open for 4% of the time, Pallas kernels for 0%

profile of v1, /device:TPU:2, one launch (start us, length us, event | category | flops | bytes accessed | tf_op | source)
XLA Modules:
  0.0 616.4 jit_solution(11347363976886414935)
XLA Ops:
  6.5 1.3 copy.25
  8.3 1.1 pad_maximum_fusion
  9.5 15.2 %all-to-all-start = ((bf16[280,16,128]{2,0,1:T(8,128)(2,1)}), bf16[280,16,128]{2,0,1:T(8,128)(2,1)S(1)}, u32[]{:S(2)}, u32[]{:S(2)}) async-start(bf16[280,16,128]{2,0,1:T(8,128)(2,1)} %pad_maximum_fusion), calls=%async_computation | async-start | bytes 2293760 | tf_op jit(solution)/shard_map/all_to_all | solution.py:58
  24.9 3.8 collective-permute-start
  29.6 2.1 pad_add_fusion
  31.7 48.9 %collective-permute-done = bf16[384,256]{0,1:T(8,128)(2,1)} collective-permute-done((bf16[384,256]{0,1:T(8,128)(2,1)S(1)}, bf16[384,256]{0,1:T(8,128)(2,1)}, u32[]{:S(2)}, u32[]{:S(2)}) %collective-permute-start) | collective-permute-done | bytes 196640 | tf_op jit(solution)/shard_map/ppermute | solution.py:66
  80.6 1.7 pad_maximum_fusion.1
  83.5 4.0 fusion.2
  87.5 3.3 fusion.3
  90.9 1.6 copy-done.2
  92.5 2.2 collective-permute-start.2
  94.8 7.8 %fusion = f32[4,384]{1,0:T(4,128)S(1)} fusion(f32[2240,384,4]{1,0,2:T(8,128)} %copy-done.2, f32[4,384]{1,0:T(4,128)S(1)} %get-tuple-element.14, pred[384,2240]{0,1:T(8,128)(4,1)S(1)} %pad_add_fusion), kind=kLoop, calls=%fused_computation.2 | loop fusion | flops 13761024 | bytes 14635008 | tf_op jit(solution)/shard_map/reduce_sum | solution.py:94
  102.6 3.6 collective-permute-start.3
  106.2 2.2 collective-permute-start.1
  108.5 3.2 collective-permute-done.1
  111.9 2.0 convolution_convert_fusion.1
  115.0 336.5 %all-gather.6.cloned.1.call-done = bf16[6144,2560]{1,0:T(8,128)(2,1)} async-done(((bf16[384,2560]{1,0:T(8,128)(2,1)}), bf16[6144,2560]{1,0:T(8,128)(2,1)}) %all-gather.6.cloned.1.call-update) | async-done | bytes 31457296 | tf_op jit(solution)/shard_map/all_gather | solution.py:13
  451.5 11.3 %reduce_sum.31 = bf16[384,2560]{1,0:T(8,128)(2,1)S(1)} reduce(bf16[16,384,2560]{2,1,0:T(8,128)(2,1)} %bitcast.64, bf16[]{:T(256)} %constant.83.clone.1), dimensions={0}, to_apply=%region_2.3 | reduce | flops 14745600 | bytes 33423362 | tf_op jit(solution)/shard_map/reduce_sum | solution.py:14
  462.8 3.7 fusion.8
  466.4 57.8 %all-gather.4.cloned.1.call-done = bf16[2560,1920]{1,0:T(8,128)(2,1)} async-done(((bf16[80,1920]{1,0:T(8,128)(2,1)}), bf16[2560,1920]{1,0:T(8,128)(2,1)}) %all-gather.4.cloned.1.call-update) | async-done | bytes 9830416 | tf_op jit(solution)/shard_map/all_gather | solution.py:124
  524.3 6.2 %fusion.6 = f32[384,1280]{1,0:T(8,128)S(1)} fusion(bf16[2560,1920]{1,0:T(8,128)(2,1)} %all-gather.4.cloned.1.call-done, bf16[384,2560]{1,0:T(8,128)(2,1)} %get-tuple-element.6, f32[2560]{0:T(1024)S(1)} %convert_element_type.56, f32[384]{0:T(512)S(1)} %add_rsqrt_fusion), kind=kOutput, calls=%fused_computation.7 | convolution fusion | flops 2520514560 | bytes 10497536 | tf_op jit(solution)/shard_map/dot_general | solution.py:130
  530.5 5.0 convolution_convert_fusion
  535.5 72.7 %reduce-scatter.2.cloned.1.call-done = bf16[24,2560]{1,0:T(8,128)(2,1)} async-done(((bf16[384,2560]{1,0:T(8,128)(2,1)}), bf16[24,2560]{1,0:T(8,128)(2,1)}) %reduce-scatter.2.cloned.1.call-update) | async-done | bytes 122896 | tf_op jit(solution)/shard_map/reduce_scatter | solution.py:140
  608.2 1.6 add_convert_fusion.1
  (58 shorter events, 3.2 us)
Async XLA Ops:
  6.5 105.3 %copy-start = (bf16[256,2560]{1,0:T(8,128)(2,1)S(1)}, bf16[256,2560]{1,0:T(8,128)(2,1)}, u32[]{:S(2)}) copy-start(bf16[256,2560]{1,0:T(8,128)(2,1)} %param.19) | copy-start | bytes 3932164
  6.5 1.4 copy-start.3
  6.5 1.7 copy-start.9
  6.5 1.7 copy-start.10
  8.1 16.6 %copy-start.5 = (bf16[384,256]{1,0:T(8,128)(2,1)S(1)}, bf16[384,256]{1,0:T(8,128)(2,1)}, u32[]{:S(2)}) copy-start(bf16[384,256]{1,0:T(8,128)(2,1)} %param.12) | copy-start | bytes 589828
  9.5 72.8 %all-to-all-start = ((bf16[280,16,128]{2,0,1:T(8,128)(2,1)}), bf16[280,16,128]{2,0,1:T(8,128)(2,1)S(1)}, u32[]{:S(2)}, u32[]{:S(2)}) async-start(bf16[280,16,128]{2,0,1:T(8,128)(2,1)} %pad_maximum_fusion), calls=%async_computation | async-start | bytes 2293760 | tf_op jit(solution)/shard_map/all_to_all | solution.py:58
  24.7 426.8 %all-gather.6.cloned.1.call-start = ((), (), s32[]{:S(2)}) async-start(), calls=%async_computation.4 | async-start | bytes 33423360 | tf_op jit(solution)/shard_map/all_gather | solution.py:13
  24.9 55.7 %collective-permute-start = (bf16[384,256]{0,1:T(8,128)(2,1)S(1)}, bf16[384,256]{0,1:T(8,128)(2,1)}, u32[]{:S(2)}, u32[]{:S(2)}) collective-permute-start(bf16[384,256]{0,1:T(8,128)(2,1)S(1)} %copy.22), channel_id=1, source_target_pairs={{0,1},{1,0},{2,3},{3,2},{4,5},{5,4},{6,7},{7,6},{8,9},{9,8},{10,11... | collective-permute-start | bytes 589832 | tf_op jit(solution)/shard_map/ppermute | solution.py:66
  83.5 4.1 copy-start.4
  87.5 5.0 copy-start.2
  92.5 19.2 %collective-permute-start.2 = (f32[2,384,128]{1,2,0:T(8,128)S(1)}, f32[2,384,128]{1,2,0:T(8,128)S(1)}, u32[]{:S(2)}, u32[]{:S(2)}) collective-permute-start(f32[2,384,128]{1,2,0:T(8,128)S(1)} %slice.63), channel_id=1, source_target_pairs={{0,1},{1,0},{2,3},{3,2},{4,5},{5,4},{6,7},{7,6},{8,9},{9,8},{10,11... | collective-permute-start | bytes 1179656 | tf_op jit(solution)/shard_map/ppermute | solution.py:98
  102.6 5.9 collective-permute-start.3
  106.2 5.5 collective-permute-start.1
  111.7 2.2 copy-start.6
  111.7 2.2 copy-start.7
  111.8 2.2 copy-start.8
  111.9 3.1 copy-start.11
  113.9 410.4 %all-gather.4.cloned.1.call-start = ((), (), s32[]{:S(2)}) async-start(), calls=%async_computation.2 | async-start | bytes 10137600 | tf_op jit(solution)/shard_map/all_gather | solution.py:124
  114.7 493.5 %reduce-scatter.2.cloned.1.call-start = ((), (), s32[]{:S(2)}) async-start(), calls=%async_computation.3 | async-start | bytes 2088960 | tf_op jit(solution)/shard_map/reduce_scatter | solution.py:140
  530.5 79.4 %copy-start.1 = (bf16[256,2560]{1,0:T(8,128)(2,1)S(1)}, bf16[256,2560]{1,0:T(8,128)(2,1)}, u32[]{:S(2)}) copy-start(bf16[256,2560]{1,0:T(8,128)(2,1)} %param.19) | copy-start | bytes 3932164
Sparse Core Ops, SparseCore 0:
  114.0 337.4 all-gather.5
  454.7 69.5 all-gather.3
  535.7 72.4 reduce-scatter.1
